TPU v7x, 256 devices: a whole 4x4x8 slice. The times are simulated.
256 devices in a mesh: dom: 32 (over y_hi, z, core), tp: 8 (over x, y_lo).
Axes of the slice: x: 4, y: 4 (y_hi: 2, y_lo: 2; y = y_hi * 2 + y_lo), z: 8, core: 2. Of those that a mesh axis runs over, the one named last changes fastest.
Arguments:
- hidden_in: bfloat16 [448, 64, 4096], P('dom', None, 'tp'), may hold values from -6 to 6
- query_weight: bfloat16 [4096, 4096], P('dom', 'tp'), may hold values from -0.09375 to 0.09375
- segment_keys: bfloat16 [448, 64, 1024], P('dom', None, 'tp'), may hold values from -6 to 6
- segment_values: bfloat16 [448, 64, 1024], P('dom', None, 'tp'), may hold values from -6 to 6
- prefix_keys: bfloat16 [32, 256, 1024], P('dom', None, 'tp'), may hold values from -80 to 80
- prefix_values: bfloat16 [32, 256, 1024], P('dom', None, 'tp'), may hold values from -6 to 6
- ancestors: int32 [448], P('dom'), may hold values from 0 to 31, as said below
- twist_weights: float32 [448], P('dom'), may hold values from 0.25 to 4
- out_grad: bfloat16 [448, 64, 4096], P('dom', None, 'tp'), may hold values from -24 to 24
Outputs:
- grad_query_weight: bfloat16 [4096, 4096], P('dom', 'tp')
- grad_segment_keys: bfloat16 [448, 64, 1024], P('dom', None, 'tp')
- grad_segment_values: bfloat16 [448, 64, 1024], P('dom', None, 'tp')
- grad_prefix_keys: float32 [32, 256, 1024], P('dom', None, 'tp')
- grad_prefix_values: float32 [32, 256, 1024], P('dom', None, 'tp')
Inputs may be any that keep to these rules, and one draw needn't show every extreme that they name: `ancestors`: among the 14 consecutive particles of one device, no ancestor is named more than 2 times, and one ancestor, the same for all devices, is named exactly 2 times on every device.
All inputs are finite; a program needn't handle non-finite values.
Results may differ from a plain program's by a relative error of at most 0.02.
The roundings to bfloat16 on the way count: a program that leaves them out, or rounds other values in their place, can miss the bound.
Values may be sent and summed in bfloat16 or wider, within the bound.
No kernel may reach another device: no remote copies, remote signals or barrier semaphores. Data moves between devices by JAX's collectives and lax.ppermute only.
A program may use at most 128 MiB of HBM per device.

v0:
```python
import math
import jax
import jax.numpy as jnp
from jax import lax
from jax.sharding import PartitionSpec as P

HD = 128


def attend(queries, scaled, seg_keys, seg_values, pre_keys, pre_values):
    factor = 1.0 / math.sqrt(queries.shape[-1])
    score_pre = (
        jnp.einsum("bikgd,bjkd->bkgij", queries, pre_keys, preferred_element_type=jnp.float32)
        * factor
    )
    score_seg = (
        jnp.einsum("bikgd,bjkd->bkgij", queries, seg_keys, preferred_element_type=jnp.float32)
        * factor
    )
    length = queries.shape[1]
    causal = lax.broadcasted_iota(jnp.int32, (length, length), 0) >= lax.broadcasted_iota(
        jnp.int32, (length, length), 1
    )
    score_seg = jnp.where(causal, score_seg, -jnp.inf)
    row_max = jnp.maximum(jnp.max(score_pre, -1), jnp.max(score_seg, -1))[..., None]
    exp_pre = jnp.exp(score_pre - row_max)
    exp_seg = jnp.exp(score_seg - row_max)
    denominator = (jnp.sum(exp_pre, -1) + jnp.sum(exp_seg, -1))[..., None]
    prob_pre = exp_pre / denominator
    prob_seg = exp_seg / denominator
    dprob_pre = jnp.einsum(
        "bikgd,bjkd->bkgij", scaled, pre_values, preferred_element_type=jnp.float32
    )
    dprob_seg = jnp.einsum(
        "bikgd,bjkd->bkgij", scaled, seg_values, preferred_element_type=jnp.float32
    )
    row_delta = (jnp.sum(prob_pre * dprob_pre, -1) + jnp.sum(prob_seg * dprob_seg, -1))[..., None]
    dscore_pre = (prob_pre * (dprob_pre - row_delta)).astype(jnp.bfloat16)
    dscore_seg = (prob_seg * (dprob_seg - row_delta)).astype(jnp.bfloat16)
    grad_q = (
        jnp.einsum("bkgij,bjkd->bikgd", dscore_pre, pre_keys, preferred_element_type=jnp.float32)
        + jnp.einsum("bkgij,bjkd->bikgd", dscore_seg, seg_keys, preferred_element_type=jnp.float32)
    ) * factor
    grad_pk = (
        jnp.einsum("bkgij,bikgd->bjkd", dscore_pre, queries, preferred_element_type=jnp.float32)
        * factor
    )
    grad_pv = jnp.einsum(
        "bkgij,bikgd->bjkd",
        prob_pre.astype(jnp.bfloat16),
        scaled,
        preferred_element_type=jnp.float32,
    )
    grad_sk = (
        jnp.einsum("bkgij,bikgd->bjkd", dscore_seg, queries, preferred_element_type=jnp.float32)
        * factor
    )
    grad_sv = jnp.einsum(
        "bkgij,bikgd->bjkd",
        prob_seg.astype(jnp.bfloat16),
        scaled,
        preferred_element_type=jnp.float32,
    )
    return (
        grad_q.astype(jnp.bfloat16),
        grad_sk.astype(jnp.bfloat16),
        grad_sv.astype(jnp.bfloat16),
        grad_pk,
        grad_pv,
    )


def local(
    hidden_in,
    query_weight,
    segment_keys,
    segment_values,
    prefix_keys,
    prefix_values,
    ancestors,
    twist_weights,
    out_grad,
):
    particles_here = hidden_in.shape[0]
    length = hidden_in.shape[1]
    owners = lax.axis_size("dom")
    features = lax.all_gather(hidden_in, "tp", axis=2, tiled=True)
    token_rows = features.reshape(particles_here * length, features.shape[2])
    width_q = query_weight.shape[1]
    width_kv = segment_keys.shape[2]
    kv_heads = width_kv // HD
    group_size = width_q // width_kv
    prefix = prefix_keys.shape[1]
    queries = jnp.dot(
        token_rows,
        lax.all_gather(query_weight, "dom", axis=0, tiled=True),
        preferred_element_type=jnp.float32,
    ).astype(jnp.bfloat16)
    queries = queries.reshape(particles_here, length, width_q)
    scaled = (out_grad.astype(jnp.float32) * twist_weights[:, None, None]).astype(jnp.bfloat16)
    own_kv = jnp.concatenate([prefix_keys, prefix_values], axis=2)
    every_kv = lax.all_to_all(
        jnp.broadcast_to(own_kv, (owners,) + own_kv.shape[1:]),
        "dom",
        split_axis=0,
        concat_axis=0,
        tiled=True,
    )
    picked = jnp.take(every_kv, ancestors, axis=0)
    pre_keys = picked[:, :, :width_kv]
    pre_values = picked[:, :, width_kv:]
    grad_q, grad_sk, grad_sv, grad_pk, grad_pv = attend(
        queries.reshape(particles_here, length, kv_heads, group_size, HD),
        scaled.reshape(particles_here, length, kv_heads, group_size, HD),
        segment_keys.reshape(particles_here, length, kv_heads, HD),
        segment_values.reshape(particles_here, length, kv_heads, HD),
        pre_keys.reshape(particles_here, prefix, kv_heads, HD),
        pre_values.reshape(particles_here, prefix, kv_heads, HD),
    )
    grad_pkv = jnp.concatenate(
        [
            grad_pk.reshape(particles_here, prefix, width_kv),
            grad_pv.reshape(particles_here, prefix, width_kv),
        ],
        axis=2,
    )
    owner_ids = jnp.arange(owners, dtype=jnp.int32)
    onehot = (owner_ids[:, None] == ancestors[None, :]).astype(jnp.float32)
    outgoing = jnp.einsum("ap,pjc->ajc", onehot, grad_pkv, precision=lax.Precision.HIGHEST)
    incoming = lax.all_to_all(outgoing, "dom", split_axis=0, concat_axis=0, tiled=True)
    summed = jnp.sum(incoming, axis=0)
    grad_pre_keys = summed[None, :, :width_kv]
    grad_pre_values = summed[None, :, width_kv:]
    grad_seg_keys = grad_sk.reshape(particles_here, length, width_kv)
    grad_seg_values = grad_sv.reshape(particles_here, length, width_kv)
    grad_rows = grad_q.reshape(particles_here * length, width_q)
    grad_weight = lax.psum_scatter(
        jnp.einsum("tc,tq->cq", token_rows, grad_rows, preferred_element_type=jnp.float32).astype(
            jnp.bfloat16
        ),
        "dom",
        scatter_dimension=0,
        tiled=True,
    )
    return (grad_weight, grad_seg_keys, grad_seg_values, grad_pre_keys, grad_pre_values)


def solution(mesh):
    return jax.shard_map(
        local,
        mesh=mesh,
        in_specs=(
            P("dom", None, "tp"),
            P("dom", "tp"),
            P("dom", None, "tp"),
            P("dom", None, "tp"),
            P("dom", None, "tp"),
            P("dom", None, "tp"),
            P("dom"),
            P("dom"),
            P("dom", None, "tp"),
        ),
        out_specs=(
            P("dom", "tp"),
            P("dom", None, "tp"),
            P("dom", None, "tp"),
            P("dom", None, "tp"),
            P("dom", None, "tp"),
        ),
        check_vma=False,
    )
```

profile of v0, /device:TPU:6, one launch (start us, length us, event | category | flops | bytes accessed | tf_op | source)
XLA Modules:
  0.0 559.1 jit_solution(17985210257255980945)
XLA Ops:
  8.7 0.9 maximum_bitcast_fusion
  9.6 2.4 broadcast_in_dim.41
  12.0 11.7 %all-to-all-start = ((bf16[32,256,256]{2,1,0:T(8,128)(2,1)}), bf16[32,256,256]{2,1,0:T(8,128)(2,1)}, u32[]{:S(2)}, u32[]{:S(2)}) async-start(bf16[32,256,256]{2,1,0:T(8,128)(2,1)} %broadcast_in_dim.41), calls=%async_computation | async-start | bytes 8388608 | tf_op jit(solution)/shard_map/all_to_all | solution.py:102
  23.8 111.2 %all-to-all-done = bf16[32,256,256]{2,1,0:T(8,128)(2,1)} async-done(((bf16[32,256,256]{2,1,0:T(8,128)(2,1)}), bf16[32,256,256]{2,1,0:T(8,128)(2,1)}, u32[]{:S(2)}, u32[]{:S(2)}) %all-to-all-start) | async-done | bytes 4194336 | tf_op jit(solution)/shard_map/all_to_all | solution.py:102
  135.0 4.2 gather_fusion
  139.2 1.7 broadcast_select_fusion
  140.9 145.1 %all-gather.3.cloned.1.call-done = bf16[14,64,4096]{2,1,0:T(8,128)(2,1)} async-done(((bf16[14,64,512]{2,1,0:T(8,128)(2,1)}), bf16[14,64,4096]{2,1,0:T(8,128)(2,1)}) %all-gather.3.cloned.1.call-update) | async-done | bytes 7340048 | tf_op jit(solution)/shard_map/all_gather | solution.py:87
  286.0 9.2 %convolution_convert_fusion.1 = bf16[896,512]{1,0:T(8,128)(2,1)} fusion(bf16[896,4096]{1,0:T(8,128)(2,1)} %bitcast.207, bf16[4096,512]{1,0:T(8,128)(2,1)} %all-gather.5.cloned.1.call-done), kind=kOutput, calls=%fused_computation.35 | convolution fusion | flops 3758555136 | bytes 12451840 | tf_op jit(solution)/shard_map/dot_general | solution.py:94
  295.2 1.9 reshape.161
  297.0 0.7 bitcast_reduce_fusion
  297.8 1.0 fusion.60
  298.9 1.2 fusion.6
  301.3 2.6 fusion.1
  303.9 2.9 fusion.20
  306.9 2.4 fusion.13
  309.3 1.8 fusion.7
  311.6 2.2 pad_maximum_fusion
  313.7 5.4 copy.47
  319.1 5.7 %fusion.55 = f32[32,256,256]{2,0,1:T(8,128)S(1)} fusion(f32[14,256,256]{2,0,1:T(8,128)} %copy.47, s32[14]{0:T(128)S(1)} %copy-done.7), kind=kOutput, calls=%fused_computation.77 | convolution fusion | flops 352321984 | bytes 12058680 | tf_op jit(solution)/shard_map/ap,pjc->ajc/dot_general | solution.py:129
  324.8 8.1 %copy.48 = f32[32,256,256]{2,1,0:T(8,128)} copy(f32[32,256,256]{2,0,1:T(8,128)S(1)} %fusion.55) | data formatting | bytes 16777216 | tf_op jit(solution)/shard_map/ap,pjc->ajc/dot_general | solution.py:129
  332.9 13.0 %all-to-all-start.1 = ((f32[32,256,256]{2,1,0:T(8,128)}), f32[32,256,256]{2,1,0:T(8,128)}, u32[]{:S(2)}, u32[]{:S(2)}) async-start(f32[32,256,256]{2,1,0:T(8,128)} %copy.48), calls=%async_computation.1 | async-start | bytes 16777216 | tf_op jit(solution)/shard_map/all_to_all | solution.py:130
  345.9 2.7 fusion.30
  348.6 0.9 copy-done.5
  350.0 1.0 copy-done.4
  351.7 0.8 copy.42
  352.5 9.5 %fusion = bf16[4096,512]{0,1:T(8,128)(2,1)} fusion(bf16[896,4096]{1,0:T(8,128)(2,1)} %bitcast.208, bf16[112,8,4,128]{3,2,1,0:T(4,128)(2,1)S(1)} %bitcast.206), kind=kOutput, calls=%fused_computation.2 | convolution fusion | flops 3760193536 | bytes 12451840 | tf_op jit(solution)/shard_map/tc,tq->cq/dot_general | solution.py:138
  362.0 6.5 %copy.59 = bf16[4096,512]{1,0:T(8,128)(2,1)} copy(bf16[4096,512]{0,1:T(8,128)(2,1)} %fusion) | data formatting | bytes 8388608
  368.5 1.2 copy-done.6
  369.6 1.1 fusion.27
  371.3 1.3 fusion.28
  372.6 175.3 %all-to-all-done.1 = f32[32,256,256]{2,1,0:T(8,128)} async-done(((f32[32,256,256]{2,1,0:T(8,128)}), f32[32,256,256]{2,1,0:T(8,128)}, u32[]{:S(2)}, u32[]{:S(2)}) %all-to-all-start.1) | async-done | bytes 8388640 | tf_op jit(solution)/shard_map/all_to_all | solution.py:130
  547.9 3.9 reduce_sum.49
  (41 shorter events, 5.6 us)
Async XLA Ops:
  7.2 290.6 %copy-start = (bf16[14,64,128]{2,1,0:T(8,128)(2,1)S(1)}, bf16[14,64,128]{2,1,0:T(8,128)(2,1)}, u32[]{:S(2)}) copy-start(bf16[14,64,128]{2,1,0:T(8,128)(2,1)} %param.11) | copy-start | bytes 688132
  7.2 133.8 %all-gather.5.cloned.1.call-start = ((), (), s32[]{:S(2)}) async-start(), calls=%async_computation.4 | async-start | bytes 4325376 | tf_op jit(solution)/shard_map/all_gather | solution.py:96
  7.9 278.1 %all-gather.3.cloned.1.call-start = ((), (), s32[]{:S(2)}) async-start(), calls=%async_computation.3 | async-start | bytes 8257536 | tf_op jit(solution)/shard_map/all_gather | solution.py:87
  12.0 11.8 %copy-start.7 = (s32[14]{0:T(128)S(1)}, s32[14]{0:T(128)}, u32[]{:S(2)}) copy-start(s32[14]{0:T(128)} %param.15) | copy-start | bytes 172
  12.0 123.0 %all-to-all-start = ((bf16[32,256,256]{2,1,0:T(8,128)(2,1)}), bf16[32,256,256]{2,1,0:T(8,128)(2,1)}, u32[]{:S(2)}, u32[]{:S(2)}) async-start(bf16[32,256,256]{2,1,0:T(8,128)(2,1)} %broadcast_in_dim.41), calls=%async_computation | async-start | bytes 8388608 | tf_op jit(solution)/shard_map/all_to_all | solution.py:102
  140.9 159.7 %copy-start.3 = (bf16[14,256,256]{2,1,0:T(8,128)(2,1)}, bf16[14,256,256]{2,1,0:T(8,128)(2,1)S(1)}, u32[]{:S(2)}) copy-start(bf16[14,256,256]{2,1,0:T(8,128)(2,1)S(1)} %broadcast_select_fusion) | copy-start | bytes 5505028
  298.8 8.1 %copy-start.1 = (f32[14,1,4,64,64]{3,4,2,0,1:T(8,128)}, f32[14,1,4,64,64]{3,4,2,0,1:T(8,128)S(1)}, u32[]{:S(2)}) copy-start(f32[14,1,4,64,64]{3,4,2,0,1:T(8,128)S(1)} %get-tuple-element.25) | copy-start | bytes 2752516
  300.1 1.2 copy-start.8
  300.1 1.2 copy-start.11
  303.9 3.0 copy-start.10
  332.9 215.0 %all-to-all-start.1 = ((f32[32,256,256]{2,1,0:T(8,128)}), f32[32,256,256]{2,1,0:T(8,128)}, u32[]{:S(2)}, u32[]{:S(2)}) async-start(f32[32,256,256]{2,1,0:T(8,128)} %copy.48), calls=%async_computation.1 | async-start | bytes 16777216 | tf_op jit(solution)/shard_map/all_to_all | solution.py:130
  345.9 206.6 %reduce-scatter.4.cloned.1.call-start = ((), (), s32[]{:S(2)}) async-start(), calls=%async_computation.5 | async-start | bytes 4325376
  348.6 0.9 copy-start.5
  349.6 1.5 copy-start.4
  368.5 1.2 copy-start.6
  368.5 2.3 copy-start.9
  369.6 1.7 copy-start.2
Sparse Core Ops, SparseCore 0:
  10.8 122.8 all-gather.4
  135.5 150.5 all-gather.2
  368.6 177.9 reduce-scatter.3
where the time goes:
time: 560 us; the launch traced here: 559 us
  waiting for transfers between devices  433 us (77%)
  matrix products  38 us (7%)
  local copies, waits for them, and re-layouts  34.3 us (6%)
  starting transfers between devices  24.9 us (4%)
  other arithmetic  14.9 us (3%)
  between operations  14 us (2%)
    all_to_all x1, waiting for transfers between devices, local(): lax.all_to_all(outgoing, 'dom', split_axis=0, concat_axis=0, tiled=True)  175 us
    all_gather x1, waiting for transfers between devices, local(): features = lax.all_gather(hidden_in, 'tp', axis=2, tiled=True)  145 us
    all_to_all x1, waiting for transfers between devices, local(): lax.all_to_all(jnp.broadcast_to(own_kv, (owners,) + own_kv.shape[1:]), 'd...  111 us
    all_to_all x1, starting transfers between devices, local(): lax.all_to_all(outgoing, 'dom', split_axis=0, concat_axis=0, tiled=True)  13 us
    all_to_all x1, starting transfers between devices, local(): lax.all_to_all(jnp.broadcast_to(own_kv, (owners,) + own_kv.shape[1:]), 'd...  11.7 us
  transfers between devices with their start and end apart: 5, of which 3 were waited for; matrix products, arithmetic and copies ran while one was open for 7% of the time, Pallas kernels for 0%

commit v1 on v0

--- a/solution.py
+++ b/solution.py
@@ -84,7 +84,15 @@
     particles_here = hidden_in.shape[0]
     length = hidden_in.shape[1]
     owners = lax.axis_size("dom")
-    features = lax.all_gather(hidden_in, "tp", axis=2, tiled=True)
+    features = jnp.concatenate(
+        lax.all_to_all(
+            jnp.stack([hidden_in for _ in range(lax.axis_size("tp"))]),
+            axis_name="tp",
+            split_axis=0,
+            concat_axis=0,
+        ),
+        axis=2,
+    )
     token_rows = features.reshape(particles_here * length, features.shape[2])
     width_q = query_weight.shape[1]
     width_kv = segment_keys.shape[2]

time: 560 us -> 490 us (0.88)
  waiting for transfers between devices: 433 us -> 349 us
  local copies, waits for them, and re-layouts: 34.3 us -> 51.5 us
    all_gather x1 -> x0, waiting for transfers between devices: 145 us -> none  [local(): features = lax.all_gather(hidden_in, 'tp', axis=2, tiled=True)]
    all_to_all x0 -> x1, waiting for transfers between devices: none -> 98.4 us  [local(): lax.all_to_all(jnp.stack([hidden_in for _ in range(lax.axis_size('tp'))])...]
    all_to_all x1, waiting for transfers between devices: 111 us -> 72 us  [local(): lax.all_to_all(jnp.broadcast_to(own_kv, (owners,) + own_kv.shape[1:]), 'd...]
    reshape x0 -> x1, local copies, waits for them, and re-layouts: none -> 8.14 us  [local(): jnp.concatenate(lax.all_to_all(jnp.stack([hidden_in for _ in range(lax.ax...]
    all_to_all x0 -> x1, starting transfers between devices: none -> 7.07 us  [local(): lax.all_to_all(jnp.stack([hidden_in for _ in range(lax.axis_size('tp'))])...]
    unnamed x25 -> x34, local copies, waits for them, and re-layouts: 10.9 us -> 17.7 us
    all_to_all x1, starting transfers between devices: 13 us -> 6.66 us  [local(): lax.all_to_all(outgoing, 'dom', split_axis=0, concat_axis=0, tiled=True)]
  transfers between devices with their start and end apart: 5 -> 5, of which waited for: 3 -> 3; matrix products, arithmetic and copies ran while one was open for 7% -> 11% of each run, Pallas kernels for 0% -> 0%
where the time goes in v1:
time: 490 us; the launch traced here: 488 us
  waiting for transfers between devices  349 us (71%)
  local copies, waits for them, and re-layouts  51.5 us (11%)
  matrix products  34.4 us (7%)
  starting transfers between devices  25.2 us (5%)
  between operations  14.4 us (3%)
  other arithmetic  12.7 us (3%)
    all_to_all x1, waiting for transfers between devices, local(): lax.all_to_all(outgoing, 'dom', split_axis=0, concat_axis=0, tiled=True)  178 us
    all_to_all x1, waiting for transfers between devices, local(): lax.all_to_all(jnp.stack([hidden_in for _ in range(lax.axis_size('tp'))])...  98.4 us
    all_to_all x1, waiting for transfers between devices, local(): lax.all_to_all(jnp.broadcast_to(own_kv, (owners,) + own_kv.shape[1:]), 'd...  72 us
    unnamed x34, local copies, waits for them, and re-layouts  17.7 us
    all_to_all x1, starting transfers between devices, local(): lax.all_to_all(jnp.broadcast_to(own_kv, (owners,) + own_kv.shape[1:]), 'd...  11.4 us
  transfers between devices with their start and end apart: 5, of which 3 were waited for; matrix products, arithmetic and copies ran while one was open for 11% of the time, Pallas kernels for 0%

profile of v1, /device:TPU:6, one launch (start us, length us, event | category | flops | bytes accessed | tf_op | source)
XLA Modules:
  0.0 487.7 jit_solution(4773126330402772522)
XLA Ops:
  7.2 5.2 %stack.2 = bf16[8,14,64,512]{3,2,1,0:T(8,128)(2,1)} broadcast(bf16[14,64,512]{2,1,0:T(8,128)(2,1)} %param.9), dimensions={1,2,3} | broadcast | bytes 8257536 | tf_op jit(solution)/shard_map/stack | solution.py:89
  12.3 7.1 %all-to-all-start.1 = ((bf16[8,14,64,512]{3,2,1,0:T(8,128)(2,1)}), bf16[8,14,64,512]{3,2,1,0:T(8,128)(2,1)}, u32[]{:S(2)}, u32[]{:S(2)}) async-start(bf16[8,14,64,512]{3,2,1,0:T(8,128)(2,1)} %stack.2), calls=%async_computation.1 | async-start | bytes 14680064 | tf_op jit(solution)/shard_map/all_to_all | solution.py:88
  20.2 98.4 %all-to-all-done.1 = bf16[8,14,64,512]{3,2,1,0:T(8,128)(2,1)} async-done(((bf16[8,14,64,512]{3,2,1,0:T(8,128)(2,1)}), bf16[8,14,64,512]{3,2,1,0:T(8,128)(2,1)}, u32[]{:S(2)}, u32[]{:S(2)}) %all-to-all-start.1) | async-done | bytes 7340064 | tf_op jit(solution)/shard_map/all_to_all | solution.py:88
  118.6 2.5 broadcast_in_dim.41
  121.1 11.4 %all-to-all-start = ((bf16[32,256,256]{2,1,0:T(8,128)(2,1)}), bf16[32,256,256]{2,1,0:T(8,128)(2,1)}, u32[]{:S(2)}, u32[]{:S(2)}) async-start(bf16[32,256,256]{2,1,0:T(8,128)(2,1)} %broadcast_in_dim.41), calls=%async_computation | async-start | bytes 8388608 | tf_op jit(solution)/shard_map/all_to_all | solution.py:110
  132.6 8.1 %copy.37 = bf16[14,64,8,512]{3,2,1,0:T(8,128)(2,1)S(1)} copy(bf16[14,64,8,512]{3,1,0,2:T(8,128)(2,1)} %bitcast.4) | data formatting | bytes 14680064 | tf_op jit(solution)/shard_map/reshape | solution.py:87
  140.7 7.8 %copy.63 = bf16[112,8,8,512]{3,1,2,0:T(8,128)(2,1)} copy(bf16[112,8,8,512]{3,2,1,0:T(8,128)(2,1)S(1)} %bitcast.209) | data formatting | bytes 14680064
  148.6 8.4 %convolution_convert_fusion.1 = bf16[896,512]{1,0:T(8,128)(2,1)S(1)} fusion(bf16[896,4096]{1,0:T(8,128)(2,1)} %bitcast.210, bf16[4096,512]{1,0:T(8,128)(2,1)} %all-gather.2.cloned.1.call-done), kind=kOutput, calls=%fused_computation.35 | convolution fusion | flops 3758555136 | bytes 12451840 | tf_op jit(solution)/shard_map/dot_general | solution.py:102
  157.2 72.0 %all-to-all-done = bf16[32,256,256]{2,1,0:T(8,128)(2,1)} async-done(((bf16[32,256,256]{2,1,0:T(8,128)(2,1)}), bf16[32,256,256]{2,1,0:T(8,128)(2,1)}, u32[]{:S(2)}, u32[]{:S(2)}) %all-to-all-start) | async-done | bytes 4194336 | tf_op jit(solution)/shard_map/all_to_all | solution.py:110
  229.2 2.9 gather_fusion
  232.3 0.7 bitcast_reduce_fusion
  233.1 1.0 fusion.60
  234.1 1.2 fusion.6
  236.5 2.6 fusion.1
  239.2 2.9 fusion.20
  242.2 2.4 fusion.13
  244.6 1.8 fusion.7
  246.9 2.2 pad_maximum_fusion
  249.0 5.4 %copy.48 = f32[14,256,256]{2,0,1:T(8,128)} copy(f32[14,256,256]{1,2,0:T(8,128)} %pad_maximum_fusion) | data formatting | bytes 7340032 | tf_op jit(solution)/shard_map/concatenate | solution.py:128
  254.4 5.7 %fusion.55 = f32[32,256,256]{2,0,1:T(8,128)S(1)} fusion(f32[14,256,256]{2,0,1:T(8,128)} %copy.48, s32[14]{0:T(128)S(1)} %copy-done.9), kind=kOutput, calls=%fused_computation.77 | convolution fusion | flops 352321984 | bytes 12058680 | tf_op jit(solution)/shard_map/ap,pjc->ajc/dot_general | solution.py:137
  260.2 8.1 %copy.49 = f32[32,256,256]{2,1,0:T(8,128)} copy(f32[32,256,256]{2,0,1:T(8,128)S(1)} %fusion.55) | data formatting | bytes 16777216 | tf_op jit(solution)/shard_map/ap,pjc->ajc/dot_general | solution.py:137
  268.3 6.7 %all-to-all-start.2 = ((f32[32,256,256]{2,1,0:T(8,128)}), f32[32,256,256]{2,1,0:T(8,128)}, u32[]{:S(2)}, u32[]{:S(2)}) async-start(f32[32,256,256]{2,1,0:T(8,128)} %copy.49), calls=%async_computation.2 | async-start | bytes 16777216 | tf_op jit(solution)/shard_map/all_to_all | solution.py:138
  275.0 2.8 fusion.30
  277.8 1.0 copy-done.5
  279.9 0.8 copy.43
  280.7 6.5 %fusion = bf16[4096,512]{0,1:T(8,128)(2,1)} fusion(bf16[896,4096]{1,0:T(8,128)(2,1)S(1)} %bitcast.213, bf16[112,8,4,128]{3,2,1,0:T(4,128)(2,1)S(1)} %bitcast.214), kind=kOutput, calls=%fused_computation.2 | convolution fusion | flops 3760193536 | bytes 12451840 | tf_op jit(solution)/shard_map/tc,tq->cq/dot_general | solution.py:146
  287.2 6.5 %copy.60 = bf16[4096,512]{1,0:T(8,128)(2,1)} copy(bf16[4096,512]{0,1:T(8,128)(2,1)} %fusion) | data formatting | bytes 8388608
  293.7 1.2 copy-done.6
  294.9 1.1 fusion.27
  296.5 1.3 fusion.28
  297.9 178.4 %all-to-all-done.2 = f32[32,256,256]{2,1,0:T(8,128)} async-done(((f32[32,256,256]{2,1,0:T(8,128)}), f32[32,256,256]{2,1,0:T(8,128)}, u32[]{:S(2)}, u32[]{:S(2)}) %all-to-all-start.2) | async-done | bytes 8388640 | tf_op jit(solution)/shard_map/all_to_all | solution.py:138
  476.2 3.9 reduce_sum.49
  (52 shorter events, 5.4 us)
Async XLA Ops:
  7.2 225.9 %copy-start = (bf16[14,64,128]{2,1,0:T(8,128)(2,1)S(1)}, bf16[14,64,128]{2,1,0:T(8,128)(2,1)}, u32[]{:S(2)}) copy-start(bf16[14,64,128]{2,1,0:T(8,128)(2,1)} %param.11) | copy-start | bytes 688132
  12.3 7.8 %copy-start.7 = (bf16[1,256,128]{2,1,0:T(8,128)(2,1)S(1)}, bf16[1,256,128]{2,1,0:T(8,128)(2,1)}, u32[]{:S(2)}) copy-start(bf16[1,256,128]{2,1,0:T(8,128)(2,1)} %param.14) | copy-start | bytes 196612
  12.3 7.8 %copy-start.8 = (bf16[1,256,128]{2,1,0:T(8,128)(2,1)S(1)}, bf16[1,256,128]{2,1,0:T(8,128)(2,1)}, u32[]{:S(2)}) copy-start(bf16[1,256,128]{2,1,0:T(8,128)(2,1)} %param.13) | copy-start | bytes 196612
  12.3 106.2 %all-to-all-start.1 = ((bf16[8,14,64,512]{3,2,1,0:T(8,128)(2,1)}), bf16[8,14,64,512]{3,2,1,0:T(8,128)(2,1)}, u32[]{:S(2)}, u32[]{:S(2)}) async-start(bf16[8,14,64,512]{3,2,1,0:T(8,128)(2,1)} %stack.2), calls=%async_computation.1 | async-start | bytes 14680064 | tf_op jit(solution)/shard_map/all_to_all | solution.py:88
  19.4 129.1 %all-gather.2.cloned.1.call-start = ((), (), s32[]{:S(2)}) async-start(), calls=%async_computation.4 | async-start | bytes 4325376 | tf_op jit(solution)/shard_map/all_gather | solution.py:104
  121.1 11.5 %copy-start.9 = (s32[14]{0:T(128)S(1)}, s32[14]{0:T(128)}, u32[]{:S(2)}) copy-start(s32[14]{0:T(128)} %param.15) | copy-start | bytes 172
  121.1 108.1 %all-to-all-start = ((bf16[32,256,256]{2,1,0:T(8,128)(2,1)}), bf16[32,256,256]{2,1,0:T(8,128)(2,1)}, u32[]{:S(2)}, u32[]{:S(2)}) async-start(bf16[32,256,256]{2,1,0:T(8,128)(2,1)} %broadcast_in_dim.41), calls=%async_computation | async-start | bytes 8388608 | tf_op jit(solution)/shard_map/all_to_all | solution.py:110
  232.3 3.5 copy-start.3
  234.1 8.1 %copy-start.1 = (f32[14,1,4,64,64]{3,4,2,0,1:T(8,128)}, f32[14,1,4,64,64]{3,4,2,0,1:T(8,128)S(1)}, u32[]{:S(2)}) copy-start(f32[14,1,4,64,64]{3,4,2,0,1:T(8,128)S(1)} %get-tuple-element.25) | copy-start | bytes 2752516
  235.4 1.2 copy-start.10
  235.4 1.2 copy-start.13
  239.2 3.0 copy-start.12
  268.3 208.0 %all-to-all-start.2 = ((f32[32,256,256]{2,1,0:T(8,128)}), f32[32,256,256]{2,1,0:T(8,128)}, u32[]{:S(2)}, u32[]{:S(2)}) async-start(f32[32,256,256]{2,1,0:T(8,128)} %copy.49), calls=%async_computation.2 | async-start | bytes 16777216 | tf_op jit(solution)/shard_map/all_to_all | solution.py:138
  274.9 206.0 %reduce-scatter.4.cloned.1.call-start = ((), (), s32[]{:S(2)}) async-start(), calls=%async_computation.5 | async-start | bytes 4325376
  275.0 4.3 copy-start.4
  275.0 5.7 %slice-start = ((s8[7340032]{0:T(1024)(128)(4,1)}), s8[4194304]{0:T(1024)(128)(4,1)S(1)}, s32[]{:S(2)}) async-start(s8[7340032]{0:T(1024)(128)(4,1)} %bitcast.211), calls=%async_computation.6 | async-start | bytes 8388608
  277.8 1.0 copy-start.5
  278.8 1.9 slice-start.1
  293.7 1.2 copy-start.6
  293.7 2.3 copy-start.11
  294.9 1.7 copy-start.2
Sparse Core Ops, SparseCore 0:
  23.0 114.5 all-gather.1
  293.9 186.6 reduce-scatter.3
